TPU v7x, 512 devices: a whole 4x4x16 slice. The times are simulated.
512 devices in a mesh: head: 8 (over x, core), expert: 64 (over z, y).
Axes of the slice: x: 4, y: 4, z: 16, core: 2. Of those that a mesh axis runs over, the one named last changes fastest.
Arguments:
- q_latent: bfloat16 [512, 64, 512], P('expert', 'head'), may hold values from -16 to 16
- q_rotary: bfloat16 [512, 64, 64], P('expert', 'head'), may hold values from -3 to 3
- cache_latent: bfloat16 [512, 128, 512], P('expert'), may hold values from -5 to 5
- cache_rotary: bfloat16 [512, 64, 128], P('expert'), may hold values from -5 to 5
- lengths: int32 [512], P('expert'), may hold values from 16 to 128, as said below
- w_value_out: bfloat16 [32768, 5120], P('head', 'expert'), may hold values from -0.25 to 0.25
- resid: bfloat16 [512, 5120], P('expert'), may hold values from -8 to 8
- norm_gain: float32 [5120], replicated, may hold values from 0.1 to 1.9
- route_ids: int32 [512, 6], P('expert'), may hold values from 0 to 63, as said below
- route_weights: float32 [512, 6], P('expert'), may hold values from 0.1 to 0.6
- w_gate_up: bfloat16 [64, 2, 768, 5120], P('expert', None, 'head'), may hold values from -0.078125 to 0.078125
- w_down: bfloat16 [64, 768, 5120], P('expert', 'head'), may hold values from -0.21875 to 0.21875
Outputs:
- mixed_out: float32 [512, 5120], P('expert', 'head')
Inputs may be any that keep to these rules, and one draw needn't show every extreme that they name: `lengths`: slots at positions below a sequence's length are valid; some sequence has length 128. `route_ids`: each row names 6 different experts. Among the rows of one device (aligned blocks of 8 rows) no expert is named by more than 2 rows, and one expert is named by exactly 2 rows in every block.
All inputs are finite; a program needn't handle non-finite values.
Results may differ from a plain program's by a relative error of at most 0.0046.
Values may be sent and summed in bfloat16 or wider, within the bound.
No kernel may reach another device: no remote copies, remote signals or barrier semaphores. Data moves between devices by JAX's collectives and lax.ppermute only.
A program may use at most 64 MiB of HBM per device.

v0:
```python
import jax
import jax.numpy as jnp
from jax import lax
from jax.sharding import Mesh
from jax.sharding import PartitionSpec as P

EXPERT = ("ez", "ey")
softmax_scale = 192.0 ** (-0.5)
norm_epsilon = 1e-06


def attend(q_latent, q_rotary, cache_latent, cache_rotary, lengths):
    scores = jnp.einsum("shl,scl->shc", q_latent, cache_latent, preferred_element_type=jnp.float32)
    scores = scores + jnp.einsum(
        "shr,src->shc", q_rotary, cache_rotary, preferred_element_type=jnp.float32
    )
    scores = scores * softmax_scale
    position = lax.broadcasted_iota(jnp.int32, scores.shape, 2)
    scores = jnp.where(position < lengths[:, None, None], scores, -1e30)
    highest = jnp.max(scores, axis=2, keepdims=True)
    weights = jnp.exp(scores - highest)
    probs = (weights / jnp.sum(weights, axis=2, keepdims=True)).astype(jnp.bfloat16)
    return jnp.einsum(
        "shc,scl->shl", probs, cache_latent, preferred_element_type=jnp.float32
    ).astype(jnp.bfloat16)


def on_device(
    q_latent,
    q_rotary,
    cache_latent,
    cache_rotary,
    lengths,
    w_value_out,
    resid,
    norm_gain,
    route_ids,
    route_weights,
    w_gate_up,
    w_down,
):
    seq_local = q_latent.shape[0]
    latent_out = attend(q_latent, q_rotary, cache_latent, cache_rotary, lengths)
    flattened = latent_out.reshape(seq_local, -1)
    z_count = lax.axis_size("ez")
    latent_copies = jnp.broadcast_to(flattened[None], (z_count,) + flattened.shape)
    gathered = lax.all_to_all(latent_copies, "ez", split_axis=0, concat_axis=0, tiled=True)
    gathered = gathered.reshape(-1, flattened.shape[1])
    value_blocks = lax.all_gather(w_value_out, "ey", axis=0, tiled=False)
    column_terms = jnp.einsum(
        "sk,jkc->sjc", gathered, value_blocks, preferred_element_type=jnp.float32
    ).reshape(gathered.shape[0], -1)
    column_sums = lax.psum(column_terms, "head")
    attention = lax.all_to_all(
        column_sums.astype(jnp.bfloat16), "ez", split_axis=0, concat_axis=1, tiled=True
    )
    stream = resid.astype(jnp.float32) + attention.astype(jnp.float32)
    mean_square = jnp.mean(stream * stream, axis=1, keepdims=True)
    normed = (stream * lax.rsqrt(mean_square + norm_epsilon) * norm_gain).astype(jnp.bfloat16)
    expert_count = lax.axis_size("ez") * lax.axis_size("ey")
    top_count = route_ids.shape[1]
    capacity = max(2, -(-(seq_local * top_count) // expert_count))
    flat_ids = route_ids.reshape(-1)
    one_hot = (flat_ids[:, None] == jnp.arange(expert_count, dtype=jnp.int32)[None, :]).astype(
        jnp.int32
    )
    earlier = jnp.cumsum(one_hot, axis=0) - one_hot
    slot_index = jnp.sum(earlier * one_hot, axis=1)
    target = (flat_ids * capacity + slot_index).reshape(seq_local, top_count)
    places = jnp.arange(expert_count * capacity, dtype=jnp.int32)
    matches = target[None, :, :] == places[:, None, None]
    selector = jnp.sum(matches.astype(jnp.int32), axis=2).astype(jnp.bfloat16)
    blending = jnp.sum(jnp.where(matches, route_weights[None, :, :], 0.0), axis=2)
    gate_up = w_gate_up[0]
    col_width = stream.shape[1] // lax.axis_size("head")
    offset = lax.axis_index("head") * col_width
    normed_cols = lax.dynamic_slice_in_dim(normed, offset, col_width, 1)
    outgoing = jnp.dot(selector, normed_cols, preferred_element_type=jnp.float32).astype(
        jnp.bfloat16
    )
    outgoing = outgoing.reshape(expert_count, capacity, -1)
    arrived = lax.all_to_all(outgoing, EXPERT, split_axis=0, concat_axis=0, tiled=True)
    arrived_cols = arrived.reshape(-1, arrived.shape[2])
    head_count = lax.axis_size("head")
    down_blocks = w_down[0].reshape(w_down.shape[1], head_count, -1)
    arrived_cols, down_blocks = lax.optimization_barrier((arrived_cols, down_blocks))
    down_cols = lax.all_to_all(down_blocks, "head", split_axis=1, concat_axis=0, tiled=True)
    down_cols = down_cols.reshape(-1, down_blocks.shape[2])
    flat_rows = lax.all_gather(arrived_cols, "head", axis=1, tiled=True)
    projected = jnp.einsum("rd,gfd->rgf", flat_rows, gate_up, preferred_element_type=jnp.float32)
    hidden = (jax.nn.silu(projected[:, 0]) * projected[:, 1]).astype(jnp.bfloat16)
    hidden_all = lax.all_gather(hidden, "head", axis=1, tiled=True)
    summed_cols = jnp.dot(hidden_all, down_cols, preferred_element_type=jnp.float32).astype(
        jnp.bfloat16
    )
    summed_rows = summed_cols.reshape(expert_count, capacity, -1)
    returned = lax.all_to_all(summed_rows, EXPERT, split_axis=0, concat_axis=0, tiled=True)
    back_rows = returned.reshape(expert_count * capacity, -1).astype(jnp.float32)
    mixture = jnp.dot(blending.T, back_rows, precision=lax.Precision.HIGHEST)
    stream_cols = lax.dynamic_slice_in_dim(stream, offset, col_width, 1)
    return stream_cols + mixture


def solution(mesh):
    placed = (
        P(EXPERT, "head", None),
        P(EXPERT, "head", None),
        P(EXPERT, None, None),
        P(EXPERT, None, None),
        P(EXPERT),
        P("head", EXPERT),
        P(EXPERT, None),
        P(),
        P(EXPERT, None),
        P(EXPERT, None),
        P(EXPERT, None, "head", None),
        P(EXPERT, "head", None),
    )
    head_count, expert_total = mesh.devices.shape
    y_count = len({device.coords[1] for device in mesh.devices[0]})
    split_mesh = Mesh(
        mesh.devices.reshape(head_count, expert_total // y_count, y_count), ("head",) + EXPERT
    )
    return jax.shard_map(
        on_device, mesh=split_mesh, in_specs=placed, out_specs=P(EXPERT, "head"), check_vma=False
    )
```

profile of v0, /device:TPU:8, one launch (start us, length us, event | category | flops | bytes accessed | tf_op | source)
XLA Modules:
  0.0 234.2 jit_solution(10736050746131402408)
XLA Ops:
  7.3 1.6 fusion.20
  8.9 1.1 fusion.8
  10.5 1.1 broadcast_in_dim.33
  11.6 15.2 %all-to-all-start = ((bf16[16,8,4096]{2,1,0:T(8,128)(2,1)}), bf16[16,8,4096]{2,1,0:T(8,128)(2,1)S(1)}, u32[]{:S(2)}, u32[]{:S(2)}) async-start(bf16[16,8,4096]{2,1,0:T(8,128)(2,1)} %broadcast_in_dim.33), calls=%async_computation | async-start | bytes 2097152 | tf_op jit(solution)/shard_map/all_to_all | solution.py:47
  27.3 28.6 %all-gather.6.cloned.1.call-done = bf16[16384,80]{0,1:T(8,128)(2,1)} async-done(((bf16[4096,80]{0,1:T(8,128)(2,1)}), bf16[16384,80]{0,1:T(8,128)(2,1)}) %all-gather.6.cloned.1.call-update) | async-done | bytes 2621456 | tf_op jit(solution)/shard_map/all_gather | solution.py:49
  55.9 5.5 %reshape.55 = bf16[4,4096,80]{1,0,2:T(4,128)(2,1)} reshape(bf16[16384,80]{0,1:T(8,128)(2,1)} %all-gather.6.cloned.1.call-done) | data formatting | bytes 5242880 | tf_op jit(solution)/shard_map/all_gather | solution.py:49
  61.4 4.7 %copy.24 = bf16[4,80,4096]{2,1,0:T(8,128)(2,1)} copy(bf16[4,80,4096]{2,0,1:T(4,128)(2,1)} %bitcast.50) | data formatting | bytes 5242880 | tf_op jit(solution)/shard_map/sk,jkc->sjc/dot_general | solution.py:50
  66.1 10.7 %all-to-all-done = bf16[16,8,4096]{2,1,0:T(8,128)(2,1)S(1)} async-done(((bf16[16,8,4096]{2,1,0:T(8,128)(2,1)}), bf16[16,8,4096]{2,1,0:T(8,128)(2,1)S(1)}, u32[]{:S(2)}, u32[]{:S(2)}) %all-to-all-start) | async-done | bytes 1048608 | tf_op jit(solution)/shard_map/all_to_all | solution.py:47
  76.8 2.6 %fusion.9 = f32[128,320]{0,1:T(8,128)S(1)} fusion(bf16[320,4096]{1,0:T(8,128)(2,1)} %bitcast.49, bf16[16,8,4096]{2,1,0:T(8,128)(2,1)S(1)} %all-to-all-done), kind=kOutput, calls=%fused_computation.14 | convolution fusion | flops 335544320 | bytes 3833856 | tf_op jit(solution)/shard_map/sk,jkc->sjc/dot_general | solution.py:50
  79.4 25.1 %all-reduce.1 = bf16[128,320]{0,1:T(8,128)(2,1)S(1)} all-reduce(f32[128,320]{0,1:T(8,128)S(1)} %fusion.9), channel_id=1, replica_groups=mesh['head'=8,'ez'=16,'ey'=4] {'head'}, use_global_device_ids=true, to_apply=%region_2.3 | all-reduce | flops 40960 | bytes 245760 | tf_op jit(solution)/shard_map/psum | solution.py:53
  105.2 10.2 %all-to-all-start.1 = ((bf16[16,8,320]{2,1,0:T(8,128)(2,1)}), bf16[16,8,320]{2,1,0:T(8,128)(2,1)S(1)}, u32[]{:S(2)}, u32[]{:S(2)}) async-start(bf16[16,8,320]{2,1,0:T(8,128)(2,1)} %bitcast.3), calls=%async_computation.1 | async-start | bytes 196608 | tf_op jit(solution)/shard_map/all_to_all | solution.py:54
  115.6 0.8 dynamic-slice
  116.4 12.1 %all-to-all-done.1 = bf16[16,8,320]{2,1,0:T(8,128)(2,1)S(1)} async-done(((bf16[16,8,320]{2,1,0:T(8,128)(2,1)}), bf16[16,8,320]{2,1,0:T(8,128)(2,1)S(1)}, u32[]{:S(2)}, u32[]{:S(2)}) %all-to-all-start.1) | async-done | bytes 81952 | tf_op jit(solution)/shard_map/all_to_all | solution.py:54
  129.9 7.0 %all-to-all-start.2 = ((bf16[64,2,640]{2,1,0:T(2,128)(2,1)}), bf16[64,2,640]{2,1,0:T(2,128)(2,1)S(1)}, u32[]{:S(2)}, u32[]{:S(2)}) async-start(bf16[64,2,640]{2,1,0:T(2,128)(2,1)} %reshape.49), calls=%async_computation.2 | async-start | bytes 327680 | tf_op jit(solution)/shard_map/all_to_all | solution.py:82
  136.9 1.3 copy.31
  138.2 14.4 %all-to-all-done.2 = bf16[64,2,640]{2,1,0:T(2,128)(2,1)S(1)} async-done(((bf16[64,2,640]{2,1,0:T(2,128)(2,1)}), bf16[64,2,640]{2,1,0:T(2,128)(2,1)S(1)}, u32[]{:S(2)}, u32[]{:S(2)}) %all-to-all-start.2) | async-done | bytes 163872 | tf_op jit(solution)/shard_map/all_to_all | solution.py:82
  153.3 1.1 copy.29
  154.4 5.0 %all-to-all-start.3 = ((bf16[96,8,640]{2,0,1:T(8,128)(2,1)}), bf16[96,8,640]{2,0,1:T(8,128)(2,1)S(1)}, u32[]{:S(2)}, u32[]{:S(2)}) async-start(bf16[96,8,640]{2,0,1:T(8,128)(2,1)} %copy.29), calls=%async_computation.3 | async-start | bytes 1966080 | tf_op jit(solution)/shard_map/all_to_all | solution.py:87
  159.4 19.3 %all-gather.4.cloned.1.call-done = bf16[128,5120]{1,0:T(8,128)(2,1)} async-done(((bf16[128,640]{1,0:T(8,128)(2,1)}), bf16[128,5120]{1,0:T(8,128)(2,1)}) %all-gather.4.cloned.1.call-update) | async-done | bytes 1310736 | tf_op jit(solution)/shard_map/all_gather | solution.py:89
  178.7 2.0 fusion.1
  180.8 12.8 %all_gather.15 = bf16[128,768]{0,1:T(8,128)(2,1)S(1)} all-gather(bf16[128,96]{0,1:T(8,128)(2,1)S(1)} %fusion.12), channel_id=1, replica_groups=mesh['head'=8,'ez'=16,'ey'=4] {'head'}, dimensions={1}, use_global_device_ids=true | all-gather | bytes 221184 | tf_op jit(solution)/shard_map/all_gather | solution.py:92
  194.6 13.5 %all-to-all-start.4 = ((bf16[64,2,640]{2,1,0:T(2,128)(2,1)}), bf16[64,2,640]{2,1,0:T(2,128)(2,1)S(1)}, u32[]{:S(2)}, u32[]{:S(2)}) async-start(bf16[64,2,640]{2,1,0:T(2,128)(2,1)} %reshape.52), calls=%async_computation.4 | async-start | bytes 327680 | tf_op jit(solution)/shard_map/all_to_all | solution.py:97
  208.3 18.2 %all-to-all-done.4 = bf16[64,2,640]{2,1,0:T(2,128)(2,1)S(1)} async-done(((bf16[64,2,640]{2,1,0:T(2,128)(2,1)}), bf16[64,2,640]{2,1,0:T(2,128)(2,1)S(1)}, u32[]{:S(2)}, u32[]{:S(2)}) %all-to-all-start.4) | async-done | bytes 163872 | tf_op jit(solution)/shard_map/all_to_all | solution.py:97
  226.6 0.8 convolution_add_fusion.1
  (41 shorter events, 6.1 us)
Async XLA Ops:
  6.5 172.2 %copy-start = (bf16[1,2,96,5120]{3,2,1,0:T(8,128)(2,1)S(1)}, bf16[1,2,96,5120]{3,2,1,0:T(8,128)(2,1)}, u32[]{:S(2)}) copy-start(bf16[1,2,96,5120]{3,2,1,0:T(8,128)(2,1)} %param.22) | copy-start | bytes 5898244
  6.5 3.6 %copy-start.1 = (bf16[8,128,512]{2,1,0:T(8,128)(2,1)S(1)}, bf16[8,128,512]{2,1,0:T(8,128)(2,1)}, u32[]{:S(2)}) copy-start(bf16[8,128,512]{2,1,0:T(8,128)(2,1)} %param.14) | copy-start | bytes 3145732
  6.5 49.3 %all-gather.6.cloned.1.call-start = ((), (), s32[]{:S(2)}) async-start(), calls=%async_computation.6 | async-start | bytes 3276800 | tf_op jit(solution)/shard_map/all_gather | solution.py:49
  10.4 16.4 %copy-start.3 = (s32[8,6]{1,0:T(8,128)S(1)}, s32[8,6]{1,0:T(8,128)}, u32[]{:S(2)}) copy-start(s32[8,6]{1,0:T(8,128)} %param.20) | copy-start | bytes 580
  11.6 65.2 %all-to-all-start = ((bf16[16,8,4096]{2,1,0:T(8,128)(2,1)}), bf16[16,8,4096]{2,1,0:T(8,128)(2,1)S(1)}, u32[]{:S(2)}, u32[]{:S(2)}) async-start(bf16[16,8,4096]{2,1,0:T(8,128)(2,1)} %broadcast_in_dim.33), calls=%async_computation | async-start | bytes 2097152 | tf_op jit(solution)/shard_map/all_to_all | solution.py:47
  76.8 51.9 %copy-start.2 = (bf16[8,5120]{1,0:T(8,128)(2,1)S(1)}, bf16[8,5120]{1,0:T(8,128)(2,1)}, u32[]{:S(2)}) copy-start(bf16[8,5120]{1,0:T(8,128)(2,1)} %param.18) | copy-start | bytes 245764
  105.2 23.2 %all-to-all-start.1 = ((bf16[16,8,320]{2,1,0:T(8,128)(2,1)}), bf16[16,8,320]{2,1,0:T(8,128)(2,1)S(1)}, u32[]{:S(2)}, u32[]{:S(2)}) async-start(bf16[16,8,320]{2,1,0:T(8,128)(2,1)} %bitcast.3), calls=%async_computation.1 | async-start | bytes 196608 | tf_op jit(solution)/shard_map/all_to_all | solution.py:54
  129.9 22.7 %all-to-all-start.2 = ((bf16[64,2,640]{2,1,0:T(2,128)(2,1)}), bf16[64,2,640]{2,1,0:T(2,128)(2,1)S(1)}, u32[]{:S(2)}, u32[]{:S(2)}) async-start(bf16[64,2,640]{2,1,0:T(2,128)(2,1)} %reshape.49), calls=%async_computation.2 | async-start | bytes 327680 | tf_op jit(solution)/shard_map/all_to_all | solution.py:82
  136.8 41.9 %all-gather.4.cloned.1.call-start = ((), (), s32[]{:S(2)}) async-start(), calls=%async_computation.5 | async-start | bytes 1474560 | tf_op jit(solution)/shard_map/all_gather | solution.py:89
  154.4 39.1 %all-to-all-start.3 = ((bf16[96,8,640]{2,0,1:T(8,128)(2,1)}), bf16[96,8,640]{2,0,1:T(8,128)(2,1)S(1)}, u32[]{:S(2)}, u32[]{:S(2)}) async-start(bf16[96,8,640]{2,0,1:T(8,128)(2,1)} %copy.29), calls=%async_computation.3 | async-start | bytes 1966080 | tf_op jit(solution)/shard_map/all_to_all | solution.py:87
  180.7 27.4 %copy-start.4 = (f32[8,6]{1,0:T(8,128)S(1)}, f32[8,6]{1,0:T(8,128)}, u32[]{:S(2)}) copy-start(f32[8,6]{1,0:T(8,128)} %param.21) | copy-start | bytes 580
  194.6 31.9 %all-to-all-start.4 = ((bf16[64,2,640]{2,1,0:T(2,128)(2,1)}), bf16[64,2,640]{2,1,0:T(2,128)(2,1)S(1)}, u32[]{:S(2)}, u32[]{:S(2)}) async-start(bf16[64,2,640]{2,1,0:T(2,128)(2,1)} %reshape.52), calls=%async_computation.4 | async-start | bytes 327680 | tf_op jit(solution)/shard_map/all_to_all | solution.py:97
Sparse Core Ops, SparseCore 0:
  9.5 46.3 all-gather.5
  153.5 25.2 all-gather.3
where the time goes:
time: 235 us; the launch traced here: 234 us
  waiting for transfers between devices  104 us (44%)
  starting transfers between devices  50.9 us (22%)
  blocking collectives  37.9 us (16%)
  local copies, waits for them, and re-layouts  18 us (8%)
  between operations  13.6 us (6%)
  matrix products  9.05 us (4%)
    all_gather x1, waiting for transfers between devices, on_device(): value_blocks = lax.all_gather(w_value_out, 'ey', axis=0, tiled=False)  28.6 us
    psum x1, blocking collectives, on_device(): column_sums = lax.psum(column_terms, 'head')  25.1 us
    all_gather x1, waiting for transfers between devices, on_device(): flat_rows = lax.all_gather(arrived_cols, 'head', axis=1, tiled=True)  19.3 us
    all_to_all x1, waiting for transfers between devices, on_device(): lax.all_to_all(summed_rows, EXPERT, split_axis=0, concat_axis=0, tiled=True)  18.2 us
    all_to_all x1, starting transfers between devices, on_device(): lax.all_to_all(latent_copies, 'ez', split_axis=0, concat_axis=0, tiled=True)  15.2 us
    all_to_all x1, waiting for transfers between devices, on_device(): lax.all_to_all(outgoing, EXPERT, split_axis=0, concat_axis=0, tiled=True)  14.4 us
    all_to_all x1, starting transfers between devices, on_device(): lax.all_to_all(summed_rows, EXPERT, split_axis=0, concat_axis=0, tiled=True)  13.5 us
    all_gather x1, blocking collectives, on_device(): hidden_all = lax.all_gather(hidden, 'head', axis=1, tiled=True)  12.8 us
  transfers between devices with their start and end apart: 7, of which 6 were waited for; matrix products, arithmetic and copies ran while one was open for 9% of the time, Pallas kernels for 0%

commit v1 on v0

--- a/solution.py
+++ b/solution.py
@@ -51,8 +51,10 @@
         "sk,jkc->sjc", gathered, value_blocks, preferred_element_type=jnp.float32
     ).reshape(gathered.shape[0], -1)
     column_sums = lax.psum(column_terms, "head")
-    attention = lax.all_to_all(
-        column_sums.astype(jnp.bfloat16), "ez", split_axis=0, concat_axis=1, tiled=True
+    body = column_sums.astype(jnp.bfloat16)
+    attention = jnp.concatenate(
+        lax.all_to_all(jnp.stack(jnp.split(body, lax.axis_size("ez"), axis=0), axis=0), "ez", 0, 0),
+        axis=1,
     )
     stream = resid.astype(jnp.float32) + attention.astype(jnp.float32)
     mean_square = jnp.mean(stream * stream, axis=1, keepdims=True)

time: 235 us -> 246 us (1.047)
  local copies, waits for them, and re-layouts: 18 us -> 28.5 us
    unnamed x13 -> x32, local copies, waits for them, and re-layouts: 1.48 us -> 10.4 us
  transfers between devices with their start and end apart: 7 -> 7, of which waited for: 6 -> 6; matrix products, arithmetic and copies ran while one was open for 9% -> 8% of each run, Pallas kernels for 0% -> 0%
where the time goes in v1:
time: 246 us; the launch traced here: 245 us
  waiting for transfers between devices  104 us (42%)
  starting transfers between devices  50.9 us (21%)
  blocking collectives  37.9 us (15%)
  local copies, waits for them, and re-layouts  28.5 us (12%)
  between operations  13.6 us (6%)
  matrix products  9.01 us (4%)
    all_gather x1, waiting for transfers between devices, on_device(): value_blocks = lax.all_gather(w_value_out, 'ey', axis=0, tiled=False)  28.6 us
    psum x1, blocking collectives, on_device(): column_sums = lax.psum(column_terms, 'head')  25.1 us
    all_gather x1, waiting for transfers between devices, on_device(): flat_rows = lax.all_gather(arrived_cols, 'head', axis=1, tiled=True)  19.3 us
    all_to_all x1, waiting for transfers between devices, on_device(): lax.all_to_all(summed_rows, EXPERT, split_axis=0, concat_axis=0, tiled=True)  18.2 us
    all_to_all x1, starting transfers between devices, on_device(): lax.all_to_all(latent_copies, 'ez', split_axis=0, concat_axis=0, tiled=True)  15.2 us
    all_to_all x1, waiting for transfers between devices, on_device(): lax.all_to_all(outgoing, EXPERT, split_axis=0, concat_axis=0, tiled=True)  14.4 us
    all_to_all x1, starting transfers between devices, on_device(): lax.all_to_all(summed_rows, EXPERT, split_axis=0, concat_axis=0, tiled=True)  13.5 us
    all_gather x1, blocking collectives, on_device(): hidden_all = lax.all_gather(hidden, 'head', axis=1, tiled=True)  12.8 us
  transfers between devices with their start and end apart: 7, of which 6 were waited for; matrix products, arithmetic and copies ran while one was open for 8% of the time, Pallas kernels for 0%

profile of v1, /device:TPU:8, one launch (start us, length us, event | category | flops | bytes accessed | tf_op | source)
XLA Modules:
  0.0 244.7 jit_solution(16344329318623246016)
XLA Ops:
  7.3 1.6 fusion.20
  8.9 1.1 fusion.8
  10.5 1.1 broadcast_in_dim.33
  11.6 15.2 %all-to-all-start = ((bf16[16,8,4096]{2,1,0:T(8,128)(2,1)}), bf16[16,8,4096]{2,1,0:T(8,128)(2,1)S(1)}, u32[]{:S(2)}, u32[]{:S(2)}) async-start(bf16[16,8,4096]{2,1,0:T(8,128)(2,1)} %broadcast_in_dim.33), calls=%async_computation | async-start | bytes 2097152 | tf_op jit(solution)/shard_map/all_to_all | solution.py:47
  27.3 28.6 %all-gather.6.cloned.1.call-done = bf16[16384,80]{0,1:T(8,128)(2,1)} async-done(((bf16[4096,80]{0,1:T(8,128)(2,1)}), bf16[16384,80]{0,1:T(8,128)(2,1)}) %all-gather.6.cloned.1.call-update) | async-done | bytes 2621456 | tf_op jit(solution)/shard_map/all_gather | solution.py:49
  55.9 5.5 %reshape.54 = bf16[4,4096,80]{1,0,2:T(4,128)(2,1)} reshape(bf16[16384,80]{0,1:T(8,128)(2,1)} %all-gather.6.cloned.1.call-done) | data formatting | bytes 5242880 | tf_op jit(solution)/shard_map/all_gather | solution.py:49
  61.4 4.7 %copy.37 = bf16[4,80,4096]{2,1,0:T(8,128)(2,1)} copy(bf16[4,80,4096]{2,0,1:T(4,128)(2,1)} %bitcast.81) | data formatting | bytes 5242880 | tf_op jit(solution)/shard_map/sk,jkc->sjc/dot_general | solution.py:50
  66.1 10.7 %all-to-all-done = bf16[16,8,4096]{2,1,0:T(8,128)(2,1)S(1)} async-done(((bf16[16,8,4096]{2,1,0:T(8,128)(2,1)}), bf16[16,8,4096]{2,1,0:T(8,128)(2,1)S(1)}, u32[]{:S(2)}, u32[]{:S(2)}) %all-to-all-start) | async-done | bytes 1048608 | tf_op jit(solution)/shard_map/all_to_all | solution.py:47
  76.8 2.6 %fusion.9 = f32[128,320]{0,1:T(8,128)S(1)} fusion(bf16[320,4096]{1,0:T(8,128)(2,1)} %bitcast.80, bf16[16,8,4096]{2,1,0:T(8,128)(2,1)S(1)} %all-to-all-done), kind=kOutput, calls=%fused_computation.14 | convolution fusion | flops 335544320 | bytes 3833856 | tf_op jit(solution)/shard_map/sk,jkc->sjc/dot_general | solution.py:50
  79.4 25.1 %all-reduce.1 = bf16[128,320]{0,1:T(8,128)(2,1)S(1)} all-reduce(f32[128,320]{0,1:T(8,128)S(1)} %fusion.9), channel_id=1, replica_groups=mesh['head'=8,'ez'=16,'ey'=4] {'head'}, use_global_device_ids=true, to_apply=%region_2.3 | all-reduce | flops 40960 | bytes 245760 | tf_op jit(solution)/shard_map/psum | solution.py:53
  115.7 10.2 %all-to-all-start.1 = ((bf16[16,8,320]{2,1,0:T(8,128)(2,1)}), bf16[16,8,320]{2,1,0:T(8,128)(2,1)S(1)}, u32[]{:S(2)}, u32[]{:S(2)}) async-start(bf16[16,8,320]{2,1,0:T(8,128)(2,1)} %constant_dynamic-update-slice_fusion), calls=%async_computation.1 | async-start | bytes 196608 | tf_op jit(solution)/shard_map/all_to_all | solution.py:56
  126.1 0.8 dynamic-slice
  126.9 12.1 %all-to-all-done.1 = bf16[16,8,320]{2,1,0:T(8,128)(2,1)S(1)} async-done(((bf16[16,8,320]{2,1,0:T(8,128)(2,1)}), bf16[16,8,320]{2,1,0:T(8,128)(2,1)S(1)}, u32[]{:S(2)}, u32[]{:S(2)}) %all-to-all-start.1) | async-done | bytes 81952 | tf_op jit(solution)/shard_map/all_to_all | solution.py:56
  140.4 7.0 %all-to-all-start.2 = ((bf16[64,2,640]{2,1,0:T(2,128)(2,1)}), bf16[64,2,640]{2,1,0:T(2,128)(2,1)S(1)}, u32[]{:S(2)}, u32[]{:S(2)}) async-start(bf16[64,2,640]{2,1,0:T(2,128)(2,1)} %reshape.48), calls=%async_computation.2 | async-start | bytes 327680 | tf_op jit(solution)/shard_map/all_to_all | solution.py:84
  147.4 1.3 copy.59
  148.7 14.4 %all-to-all-done.2 = bf16[64,2,640]{2,1,0:T(2,128)(2,1)S(1)} async-done(((bf16[64,2,640]{2,1,0:T(2,128)(2,1)}), bf16[64,2,640]{2,1,0:T(2,128)(2,1)S(1)}, u32[]{:S(2)}, u32[]{:S(2)}) %all-to-all-start.2) | async-done | bytes 163872 | tf_op jit(solution)/shard_map/all_to_all | solution.py:84
  163.8 1.1 copy.57
  164.9 5.0 %all-to-all-start.3 = ((bf16[96,8,640]{2,0,1:T(8,128)(2,1)}), bf16[96,8,640]{2,0,1:T(8,128)(2,1)S(1)}, u32[]{:S(2)}, u32[]{:S(2)}) async-start(bf16[96,8,640]{2,0,1:T(8,128)(2,1)} %copy.57), calls=%async_computation.3 | async-start | bytes 1966080 | tf_op jit(solution)/shard_map/all_to_all | solution.py:89
  169.9 19.3 %all-gather.4.cloned.1.call-done = bf16[128,5120]{1,0:T(8,128)(2,1)} async-done(((bf16[128,640]{1,0:T(8,128)(2,1)}), bf16[128,5120]{1,0:T(8,128)(2,1)}) %all-gather.4.cloned.1.call-update) | async-done | bytes 1310736 | tf_op jit(solution)/shard_map/all_gather | solution.py:91
  189.2 2.0 fusion.1
  191.3 12.8 %all_gather.15 = bf16[128,768]{0,1:T(8,128)(2,1)S(1)} all-gather(bf16[128,96]{0,1:T(8,128)(2,1)S(1)} %fusion.12), channel_id=1, replica_groups=mesh['head'=8,'ez'=16,'ey'=4] {'head'}, dimensions={1}, use_global_device_ids=true | all-gather | bytes 221184 | tf_op jit(solution)/shard_map/all_gather | solution.py:94
  205.1 13.5 %all-to-all-start.4 = ((bf16[64,2,640]{2,1,0:T(2,128)(2,1)}), bf16[64,2,640]{2,1,0:T(2,128)(2,1)S(1)}, u32[]{:S(2)}, u32[]{:S(2)}) async-start(bf16[64,2,640]{2,1,0:T(2,128)(2,1)} %reshape.51), calls=%async_computation.4 | async-start | bytes 327680 | tf_op jit(solution)/shard_map/all_to_all | solution.py:99
  218.8 18.2 %all-to-all-done.4 = bf16[64,2,640]{2,1,0:T(2,128)(2,1)S(1)} async-done(((bf16[64,2,640]{2,1,0:T(2,128)(2,1)}), bf16[64,2,640]{2,1,0:T(2,128)(2,1)S(1)}, u32[]{:S(2)}, u32[]{:S(2)}) %all-to-all-start.4) | async-done | bytes 163872 | tf_op jit(solution)/shard_map/all_to_all | solution.py:99
  237.1 0.8 convolution_add_fusion.1
  (77 shorter events, 16.6 us)
Async XLA Ops:
  6.5 182.7 %copy-start = (bf16[1,2,96,5120]{3,2,1,0:T(8,128)(2,1)S(1)}, bf16[1,2,96,5120]{3,2,1,0:T(8,128)(2,1)}, u32[]{:S(2)}) copy-start(bf16[1,2,96,5120]{3,2,1,0:T(8,128)(2,1)} %param.22) | copy-start | bytes 5898244
  6.5 3.6 %copy-start.1 = (bf16[8,128,512]{2,1,0:T(8,128)(2,1)S(1)}, bf16[8,128,512]{2,1,0:T(8,128)(2,1)}, u32[]{:S(2)}) copy-start(bf16[8,128,512]{2,1,0:T(8,128)(2,1)} %param.14) | copy-start | bytes 3145732
  6.5 49.3 %all-gather.6.cloned.1.call-start = ((), (), s32[]{:S(2)}) async-start(), calls=%async_computation.6 | async-start | bytes 3276800 | tf_op jit(solution)/shard_map/all_gather | solution.py:49
  10.4 16.4 %copy-start.5 = (s32[8,6]{1,0:T(8,128)S(1)}, s32[8,6]{1,0:T(8,128)}, u32[]{:S(2)}) copy-start(s32[8,6]{1,0:T(8,128)} %param.20) | copy-start | bytes 580
  11.6 65.2 %all-to-all-start = ((bf16[16,8,4096]{2,1,0:T(8,128)(2,1)}), bf16[16,8,4096]{2,1,0:T(8,128)(2,1)S(1)}, u32[]{:S(2)}, u32[]{:S(2)}) async-start(bf16[16,8,4096]{2,1,0:T(8,128)(2,1)} %broadcast_in_dim.33), calls=%async_computation | async-start | bytes 2097152 | tf_op jit(solution)/shard_map/all_to_all | solution.py:47
  104.9 34.3 %copy-start.2 = (bf16[8,5120]{1,0:T(8,128)(2,1)S(1)}, bf16[8,5120]{1,0:T(8,128)(2,1)}, u32[]{:S(2)}) copy-start(bf16[8,5120]{1,0:T(8,128)(2,1)} %param.18) | copy-start | bytes 245764
  115.7 23.2 %all-to-all-start.1 = ((bf16[16,8,320]{2,1,0:T(8,128)(2,1)}), bf16[16,8,320]{2,1,0:T(8,128)(2,1)S(1)}, u32[]{:S(2)}, u32[]{:S(2)}) async-start(bf16[16,8,320]{2,1,0:T(8,128)(2,1)} %constant_dynamic-update-slice_fusion), calls=%async_computation.1 | async-start | bytes 196608 | tf_op jit(solution)/shard_map/all_to_all | solution.py:56
  126.1 12.9 %copy-start.3 = (s32[8,6]{0,1:T(8,128)}, s32[8,6]{0,1:T(8,128)S(1)}, u32[]{:S(2)}) copy-start(s32[8,6]{0,1:T(8,128)S(1)} %copy.55) | copy-start | bytes 580
  140.4 22.7 %all-to-all-start.2 = ((bf16[64,2,640]{2,1,0:T(2,128)(2,1)}), bf16[64,2,640]{2,1,0:T(2,128)(2,1)S(1)}, u32[]{:S(2)}, u32[]{:S(2)}) async-start(bf16[64,2,640]{2,1,0:T(2,128)(2,1)} %reshape.48), calls=%async_computation.2 | async-start | bytes 327680 | tf_op jit(solution)/shard_map/all_to_all | solution.py:84
  147.3 41.9 %all-gather.4.cloned.1.call-start = ((), (), s32[]{:S(2)}) async-start(), calls=%async_computation.5 | async-start | bytes 1474560 | tf_op jit(solution)/shard_map/all_gather | solution.py:91
  164.9 39.1 %all-to-all-start.3 = ((bf16[96,8,640]{2,0,1:T(8,128)(2,1)}), bf16[96,8,640]{2,0,1:T(8,128)(2,1)S(1)}, u32[]{:S(2)}, u32[]{:S(2)}) async-start(bf16[96,8,640]{2,0,1:T(8,128)(2,1)} %copy.57), calls=%async_computation.3 | async-start | bytes 1966080 | tf_op jit(solution)/shard_map/all_to_all | solution.py:89
  191.2 27.4 %copy-start.6 = (f32[8,6]{1,0:T(8,128)S(1)}, f32[8,6]{1,0:T(8,128)}, u32[]{:S(2)}) copy-start(f32[8,6]{1,0:T(8,128)} %param.21) | copy-start | bytes 580
  191.2 27.5 %copy-start.4 = (s32[8,6]{0,1:T(8,128)S(1)}, s32[8,6]{0,1:T(8,128)}, u32[]{:S(2)}) copy-start(s32[8,6]{0,1:T(8,128)} %copy-done.3) | copy-start | bytes 580
  205.1 31.9 %all-to-all-start.4 = ((bf16[64,2,640]{2,1,0:T(2,128)(2,1)}), bf16[64,2,640]{2,1,0:T(2,128)(2,1)S(1)}, u32[]{:S(2)}, u32[]{:S(2)}) async-start(bf16[64,2,640]{2,1,0:T(2,128)(2,1)} %reshape.51), calls=%async_computation.4 | async-start | bytes 327680 | tf_op jit(solution)/shard_map/all_to_all | solution.py:99
Sparse Core Ops, SparseCore 0:
  9.5 46.3 all-gather.5
  164.0 25.2 all-gather.3
